TPU v7x, 256 devices: a whole 4x4x8 slice. The times are simulated.
256 devices in a mesh: ctx: 64 (over x, z, core), tp: 4 (over y).
Axes of the slice: x: 4, y: 4, z: 8, core: 2. Of those that a mesh axis runs over, the one named last changes fastest.
Arguments:
- inputs: bfloat16 [8192, 4096], P('ctx'), may hold values from -6 to 6
- w_query: bfloat16 [4096, 4096], P(None, 'tp'), may hold values from -0.109375 to 0.109375
- w_key: bfloat16 [4096, 512], P(None, 'tp'), may hold values from -0.109375 to 0.109375
- w_value: bfloat16 [4096, 512], P(None, 'tp'), may hold values from -0.09375 to 0.09375
- attn_out: bfloat16 [8192, 4096], P('ctx', 'tp'), may hold values from -6 to 6
- d_out: bfloat16 [8192, 4096], P('ctx', 'tp'), may hold values from -6 to 6
- block_order: int32 [128], replicated, may hold values from 0 to 127, each once
Outputs:
- d_input: bfloat16 [8192, 4096], P('ctx', 'tp')
Inputs may be any that keep to these rules, and one draw needn't show every extreme that they name: `block_order`: a permutation of the sequence blocks.
All inputs are finite; a program needn't handle non-finite values.
Results may differ from a plain program's by a relative error of at most 0.012.
Values may be sent and summed in bfloat16 or wider, within the bound.
No kernel may reach another device: no remote copies, remote signals or barrier semaphores. Data moves between devices by JAX's collectives and lax.ppermute only.
A program may use at most 192 MiB of HBM per device.

v0:
```python
import math
import jax
import jax.numpy as jnp
from jax import lax
from jax.sharding import PartitionSpec as P

big_negative = -1e30


def row_positions(order, start, count, span):
    rows = start + lax.iota(jnp.int32, count)
    slot = rows // span
    table = jnp.sum(
        jnp.where(slot[:, None] == lax.iota(jnp.int32, order.shape[0])[None, :], order[None, :], 0),
        axis=1,
    )
    return table * span + rows % span


def contract_rows(left, weight):
    return lax.dot_general(
        left, weight, (((1,), (1,)), ((), ())), preferred_element_type=jnp.float32
    )


def on_device(inputs, w_query, w_key, w_value, attn_out, d_out, block_order):
    tokens = inputs.shape[0]
    span = tokens // 2
    head_dim = w_key.shape[1]
    heads = w_query.shape[1] // head_dim
    scale = head_dim ** (-0.5)
    keys = jnp.dot(inputs, w_key, preferred_element_type=jnp.float32).astype(jnp.bfloat16)
    values = jnp.dot(inputs, w_value, preferred_element_type=jnp.float32).astype(jnp.bfloat16)
    seq = tokens * lax.axis_size("ctx")
    my_pos = row_positions(block_order, lax.axis_index("ctx") * tokens, tokens, span)
    latest = jnp.max(my_pos)
    queries = (
        jnp.dot(inputs, w_query, preferred_element_type=jnp.float32)
        .astype(jnp.bfloat16)
        .reshape(tokens, heads, head_dim)
    )
    grads3 = d_out.reshape(tokens, heads, head_dim)
    delta = jnp.sum(
        grads3.astype(jnp.float32) * attn_out.reshape(tokens, heads, head_dim).astype(jnp.float32),
        axis=-1,
    ).T

    def guarded(work, carry, piece_k, start):
        key_pos = row_positions(block_order, start, piece_k.shape[0], span)
        return lax.cond(jnp.min(key_pos) > latest, lambda c: c, lambda c: work(c, key_pos), carry)

    def stats_step(carry, piece_k, start):

        def work(state, key_pos):
            top, total = state
            mask = (key_pos[None, :] <= my_pos[:, None])[None]
            s = (
                jnp.einsum("thd,nd->htn", queries, piece_k, preferred_element_type=jnp.float32)
                * scale
            )
            s = jnp.where(mask, s, big_negative)
            top_new = jnp.maximum(top, jnp.max(s, axis=-1))
            terms = jnp.where(mask, jnp.exp(s - top_new[..., None]), 0.0)
            return (top_new, total * jnp.exp(top - top_new) + jnp.sum(terms, axis=-1))

        return guarded(work, carry, piece_k, start)

    def grad_step(carry, pieces, start):
        piece_k, piece_v = pieces

        def work(state, key_pos):
            dq, dk_full, dv_full = state
            mask = (key_pos[None, :] <= my_pos[:, None])[None]
            s = (
                jnp.einsum("thd,nd->htn", queries, piece_k, preferred_element_type=jnp.float32)
                * scale
            )
            p = jnp.where(mask, jnp.exp(s - lse[..., None]), 0.0)
            dp = jnp.einsum("thd,nd->htn", grads3, piece_v, preferred_element_type=jnp.float32)
            ds_b = (p * (dp - delta[..., None]) * scale).astype(jnp.bfloat16)
            p_b = p.astype(jnp.bfloat16)
            dq = dq + jnp.einsum("htn,nd->thd", ds_b, piece_k, preferred_element_type=jnp.float32)
            dk_piece = jnp.einsum("htn,thd->nd", ds_b, queries, preferred_element_type=jnp.float32)
            dv_piece = jnp.einsum("htn,thd->nd", p_b, grads3, preferred_element_type=jnp.float32)
            dk_full = lax.dynamic_update_slice_in_dim(dk_full, dk_piece, start, 0)
            dv_full = lax.dynamic_update_slice_in_dim(dv_full, dv_piece, start, 0)
            return (dq, dk_full, dv_full)

        return guarded(work, carry, piece_k, start)

    stats_init = (
        jnp.full((heads, tokens), big_negative, jnp.float32),
        jnp.zeros((heads, tokens), jnp.float32),
    )
    zero_rows = jnp.zeros((seq, head_dim), jnp.float32)
    grad_init = (jnp.zeros((tokens, heads, head_dim), jnp.float32), zero_rows, zero_rows)
    all_keys, all_values = (
        lax.all_gather(keys, "ctx", axis=0, tiled=True),
        lax.all_gather(values, "ctx", axis=0, tiled=True),
    )
    block = math.gcd(seq, 1024)
    count = seq // block

    def stats_loop(i, state):
        start = (i * block).astype(jnp.int32)
        return stats_step(state, lax.dynamic_slice_in_dim(all_keys, start, block, 0), start)

    top, total = lax.fori_loop(0, count, stats_loop, stats_init)
    lse = top + jnp.log(total)

    def grad_loop(i, state):
        start = (i * block).astype(jnp.int32)
        pieces = (
            lax.dynamic_slice_in_dim(all_keys, start, block, 0),
            lax.dynamic_slice_in_dim(all_values, start, block, 0),
        )
        return grad_step(state, pieces, start)

    dq, dk_full, dv_full = lax.fori_loop(0, count, grad_loop, grad_init)
    dk_mine, dv_mine = (
        lax.psum_scatter(dk_full, "ctx", scatter_dimension=0, tiled=True),
        lax.psum_scatter(dv_full, "ctx", scatter_dimension=0, tiled=True),
    )
    dq_b = dq.astype(jnp.bfloat16).reshape(tokens, heads * head_dim)
    partial_value = contract_rows(dq_b, w_query)
    partial_value = partial_value + contract_rows(dk_mine.astype(jnp.bfloat16), w_key)
    partial_value = partial_value + contract_rows(dv_mine.astype(jnp.bfloat16), w_value)
    return lax.psum_scatter(
        partial_value.astype(jnp.bfloat16), "tp", scatter_dimension=1, tiled=True
    )


def solution(mesh):
    placed = (
        P("ctx", None),
        P(None, "tp"),
        P(None, "tp"),
        P(None, "tp"),
        P("ctx", "tp"),
        P("ctx", "tp"),
        P(),
    )
    return jax.shard_map(
        on_device, mesh=mesh, in_specs=placed, out_specs=P("ctx", "tp"), check_vma=False
    )
```

profile of v0, /device:TPU:2, one launch (start us, length us, event | category | flops | bytes accessed | tf_op | source)
XLA Modules:
  0.0 588.8 jit_solution(3103527456440463668)
XLA Ops:
  10.3 2.6 convolution_convert_fusion.1
  13.6 4.6 fusion.47
  19.2 70.6 %all-gather.3.cloned.1.call-done = bf16[8192,128]{1,0:T(8,128)(2,1)} async-done(((bf16[128,128]{1,0:T(8,128)(2,1)}), bf16[8192,128]{1,0:T(8,128)(2,1)}) %all-gather.3.cloned.1.call-update) | async-done | bytes 2097168 | tf_op jit(solution)/shard_map/all_gather | solution.py:98
  89.7 42.9 %while.36 = (s32[]{:T(128)}, f32[8,128]{1,0:T(8,128)S(1)}, f32[8,128]{1,0:T(8,128)S(1)}, s32[128]{0:T(128)S(1)}, s32[]{:T(128)}, /*index=5*/s32[128]{0:T(128)S(1...) while((s32[]{:T(128)}, f32[8,128]{1,0:T(8,128)S(1)}, ...), condition=%wide.region_9.10_spmd, body=%wide.region_2.9_spmd.sunk | while | flops 277381120 | bytes 9385225 | solution.py:108
  92.1 3.0 conditional.4
  97.4 3.0 conditional.4
  102.8 3.0 conditional.4
  108.1 3.0 conditional.4
  113.5 3.0 conditional.4
  118.9 3.0 conditional.4
  124.2 3.0 conditional.4
  129.6 3.0 conditional.4
  132.6 34.9 %all-gather.5.cloned.1.call-done = bf16[8192,128]{1,0:T(8,128)(2,1)} async-done(((bf16[128,128]{1,0:T(8,128)(2,1)}), bf16[8192,128]{1,0:T(8,128)(2,1)}) %all-gather.5.cloned.1.call-update) | async-done | bytes 2097168 | tf_op jit(solution)/shard_map/all_gather | solution.py:99
  172.0 92.8 %while.37 = (s32[]{:T(128)}, f32[128,8,128]{2,0,1:T(8,128)S(1)}, f32[8192,128]{1,0:T(8,128)}, f32[8192,128]{1,0:T(8,128)}, s32[128]{0:T(128)S(1)}, /*index=5*/s3...) while((s32[]{:T(128)}, f32[128,8,128]{2,0,1:T(8,128)S(1)}, ...), condition=%wide.region_16.17_spmd, body=%wide.region_11.16_spmd.sunk | while | flops 1354397696 | bytes 23238016 | solution.py:119
  174.4 9.2 %conditional.5 = ((f32[128,8,128]{2,0,1:T(8,128)S(1)}, f32[8192,128]{1,0:T(8,128)}, f32[8192,128]{1,0:T(8,128)})) conditional(s32[]{:T(128)} %convert_element_type.94, (s32[1024]{0:T(1024)S(1)}, s32[128]{0:T(128)S(1)}, s32[]{:T(128)}, bf16[8192,128]{1,0:T(8,128)(2,1)}, bf16[128,8,128]{2,0,1:T(8,128)(2,1)S(1)}, /*index=5*/f32[8,128]{1,0:T(8,128)S(1)}, ...), branch_computations={%region_14.14_spmd, %region_15.15_spmd} | conditional | flops 1353973760 | bytes 23216726 | solution.py:50
  176.3 2.5 fusion.13
  185.9 9.3 %conditional.5 = ((f32[128,8,128]{2,0,1:T(8,128)S(1)}, f32[8192,128]{1,0:T(8,128)}, f32[8192,128]{1,0:T(8,128)})) conditional(s32[]{:T(128)} %convert_element_type.94, (s32[1024]{0:T(1024)S(1)}, s32[128]{0:T(128)S(1)}, s32[]{:T(128)}, bf16[8192,128]{1,0:T(8,128)(2,1)}, bf16[128,8,128]{2,0,1:T(8,128)(2,1)S(1)}, /*index=5*/f32[8,128]{1,0:T(8,128)S(1)}, ...), branch_computations={%region_14.14_spmd, %region_15.15_spmd} | conditional | flops 1353973760 | bytes 23216726 | solution.py:50
  197.5 9.3 %conditional.5 = ((f32[128,8,128]{2,0,1:T(8,128)S(1)}, f32[8192,128]{1,0:T(8,128)}, f32[8192,128]{1,0:T(8,128)})) conditional(s32[]{:T(128)} %convert_element_type.94, (s32[1024]{0:T(1024)S(1)}, s32[128]{0:T(128)S(1)}, s32[]{:T(128)}, bf16[8192,128]{1,0:T(8,128)(2,1)}, bf16[128,8,128]{2,0,1:T(8,128)(2,1)S(1)}, /*index=5*/f32[8,128]{1,0:T(8,128)S(1)}, ...), branch_computations={%region_14.14_spmd, %region_15.15_spmd} | conditional | flops 1353973760 | bytes 23216726 | solution.py:50
  199.4 2.5 fusion.13
  209.1 9.3 %conditional.5 = ((f32[128,8,128]{2,0,1:T(8,128)S(1)}, f32[8192,128]{1,0:T(8,128)}, f32[8192,128]{1,0:T(8,128)})) conditional(s32[]{:T(128)} %convert_element_type.94, (s32[1024]{0:T(1024)S(1)}, s32[128]{0:T(128)S(1)}, s32[]{:T(128)}, bf16[8192,128]{1,0:T(8,128)(2,1)}, bf16[128,8,128]{2,0,1:T(8,128)(2,1)S(1)}, /*index=5*/f32[8,128]{1,0:T(8,128)S(1)}, ...), branch_computations={%region_14.14_spmd, %region_15.15_spmd} | conditional | flops 1353973760 | bytes 23216726 | solution.py:50
  211.0 2.5 fusion.13
  220.8 9.3 %conditional.5 = ((f32[128,8,128]{2,0,1:T(8,128)S(1)}, f32[8192,128]{1,0:T(8,128)}, f32[8192,128]{1,0:T(8,128)})) conditional(s32[]{:T(128)} %convert_element_type.94, (s32[1024]{0:T(1024)S(1)}, s32[128]{0:T(128)S(1)}, s32[]{:T(128)}, bf16[8192,128]{1,0:T(8,128)(2,1)}, bf16[128,8,128]{2,0,1:T(8,128)(2,1)S(1)}, /*index=5*/f32[8,128]{1,0:T(8,128)S(1)}, ...), branch_computations={%region_14.14_spmd, %region_15.15_spmd} | conditional | flops 1353973760 | bytes 23216726 | solution.py:50
  222.6 2.5 fusion.13
  232.3 9.3 %conditional.5 = ((f32[128,8,128]{2,0,1:T(8,128)S(1)}, f32[8192,128]{1,0:T(8,128)}, f32[8192,128]{1,0:T(8,128)})) conditional(s32[]{:T(128)} %convert_element_type.94, (s32[1024]{0:T(1024)S(1)}, s32[128]{0:T(128)S(1)}, s32[]{:T(128)}, bf16[8192,128]{1,0:T(8,128)(2,1)}, bf16[128,8,128]{2,0,1:T(8,128)(2,1)S(1)}, /*index=5*/f32[8,128]{1,0:T(8,128)S(1)}, ...), branch_computations={%region_14.14_spmd, %region_15.15_spmd} | conditional | flops 1353973760 | bytes 23216726 | solution.py:50
  244.0 9.2 %conditional.5 = ((f32[128,8,128]{2,0,1:T(8,128)S(1)}, f32[8192,128]{1,0:T(8,128)}, f32[8192,128]{1,0:T(8,128)})) conditional(s32[]{:T(128)} %convert_element_type.94, (s32[1024]{0:T(1024)S(1)}, s32[128]{0:T(128)S(1)}, s32[]{:T(128)}, bf16[8192,128]{1,0:T(8,128)(2,1)}, bf16[128,8,128]{2,0,1:T(8,128)(2,1)S(1)}, /*index=5*/f32[8,128]{1,0:T(8,128)S(1)}, ...), branch_computations={%region_14.14_spmd, %region_15.15_spmd} | conditional | flops 1353973760 | bytes 23216726 | solution.py:50
  245.9 2.5 fusion.13
  255.5 9.3 %conditional.5 = ((f32[128,8,128]{2,0,1:T(8,128)S(1)}, f32[8192,128]{1,0:T(8,128)}, f32[8192,128]{1,0:T(8,128)})) conditional(s32[]{:T(128)} %convert_element_type.94, (s32[1024]{0:T(1024)S(1)}, s32[128]{0:T(128)S(1)}, s32[]{:T(128)}, bf16[8192,128]{1,0:T(8,128)(2,1)}, bf16[128,8,128]{2,0,1:T(8,128)(2,1)S(1)}, /*index=5*/f32[8,128]{1,0:T(8,128)S(1)}, ...), branch_computations={%region_14.14_spmd, %region_15.15_spmd} | conditional | flops 1353973760 | bytes 23216726 | solution.py:50
  265.8 7.7 %fusion.58 = f32[128,4096]{1,0:T(8,128)} fusion(bf16[128,1024]{0,1:T(8,128)(2,1)S(1)} %bitcast.85, bf16[4096,1024]{1,0:T(8,128)(2,1)} %param.16), kind=kOutput, calls=%fused_computation.93 | convolution fusion | flops 1073741824 | bytes 10747904 | tf_op jit(solution)/shard_map/dot_general | solution.py:21
  273.5 133.5 %reduce-scatter.4.cloned.1.call-done = f32[128,128]{1,0:T(8,128)} async-done(((f32[8192,128]{1,0:T(8,128)}), f32[128,128]{1,0:T(8,128)}) %reduce-scatter.4.cloned.1.call-update) | async-done | bytes 65552 | tf_op jit(solution)/shard_map/reduce_scatter | solution.py:121
  409.1 144.7 %reduce-scatter.6.cloned.1.call-done = f32[128,128]{1,0:T(8,128)} async-done(((f32[8192,128]{1,0:T(8,128)}), f32[128,128]{1,0:T(8,128)}) %reduce-scatter.6.cloned.1.call-update) | async-done | bytes 65552 | tf_op jit(solution)/shard_map/reduce_scatter | solution.py:122
  553.8 2.7 fusion.46
  556.5 25.7 %reduce-scatter.8.cloned.1.call-done = bf16[128,1024]{1,0:T(8,128)(2,1)} async-done(((bf16[128,4096]{1,0:T(8,128)(2,1)}), bf16[128,1024]{1,0:T(8,128)(2,1)}) %reduce-scatter.8.cloned.1.call-update) | async-done | bytes 262160 | tf_op jit(solution)/shard_map/reduce_scatter | solution.py:128
  (176 shorter events, 115.1 us)
Async XLA Ops:
  6.5 1.4 copy-start
  6.5 7.0 %copy-start.1 = (bf16[128,4096]{1,0:T(8,128)(2,1)S(1)}, bf16[128,4096]{1,0:T(8,128)(2,1)}, u32[]{:S(2)}) copy-start(bf16[128,4096]{1,0:T(8,128)(2,1)} %param.15) | copy-start | bytes 3145732
  6.5 6.4 %copy-start.2 = (bf16[128,1024]{1,0:T(8,128)(2,1)S(1)}, bf16[128,1024]{1,0:T(8,128)(2,1)}, u32[]{:S(2)}) copy-start(bf16[128,1024]{1,0:T(8,128)(2,1)} %param.20) | copy-start | bytes 786436
  6.5 6.8 %copy-start.3 = (bf16[128,1024]{1,0:T(8,128)(2,1)S(1)}, bf16[128,1024]{1,0:T(8,128)(2,1)}, u32[]{:S(2)}) copy-start(bf16[128,1024]{1,0:T(8,128)(2,1)} %param.19) | copy-start | bytes 786436
  6.5 83.2 %all-gather.3.cloned.1.call-start = ((), (), s32[]{:S(2)}) async-start(), calls=%async_computation.3 | async-start | bytes 2129920 | tf_op jit(solution)/shard_map/all_gather | solution.py:98
  10.2 157.4 %all-gather.5.cloned.1.call-start = ((), (), s32[]{:S(2)}) async-start(), calls=%async_computation.4 | async-start | bytes 2129920 | tf_op jit(solution)/shard_map/all_gather | solution.py:99
  12.8 394.2 %reduce-scatter.4.cloned.1.call-start = ((), (), s32[]{:S(2)}) async-start(), calls=%async_computation.5 | async-start | bytes 4259840 | tf_op jit(solution)/shard_map/reduce_scatter | solution.py:121
  13.6 4.7 copy-start.4
  264.8 289.0 %reduce-scatter.6.cloned.1.call-start = ((), (), s32[]{:S(2)}) async-start(), calls=%async_computation.6 | async-start | bytes 4259840 | tf_op jit(solution)/shard_map/reduce_scatter | solution.py:122
  265.4 316.9 %reduce-scatter.8.cloned.1.call-start = ((), (), s32[]{:S(2)}) async-start(), calls=%async_computation.7 | async-start | bytes 1310720 | tf_op jit(solution)/shard_map/reduce_scatter | solution.py:128
Sparse Core Ops, SparseCore 0:
  10.3 79.3 all-gather.2
  92.5 75.0 all-gather.4
  264.9 142.0 reduce-scatter.3
  411.0 142.7 reduce-scatter.5
  556.7 25.5 reduce-scatter.7
where the time goes:
time: 590 us; the launch traced here: 589 us
  waiting for transfers between devices  410 us (69%)
  matrix products  108 us (18%)
  other arithmetic  29.7 us (5%)
  loops' own time  21 us (4%)
  between operations  13.3 us (2%)
  local copies, waits for them, and re-layouts  6.58 us (1%)
    reduce_scatter x1, waiting for transfers between devices, on_device(): lax.psum_scatter(dv_full, 'ctx', scatter_dimension=0, tiled=True)  145 us
    reduce_scatter x1, waiting for transfers between devices, on_device(): lax.psum_scatter(dk_full, 'ctx', scatter_dimension=0, tiled=True)  134 us
    all_gather x1, waiting for transfers between devices, on_device(): lax.all_gather(keys, 'ctx', axis=0, tiled=True)  70.6 us
    all_gather x1, waiting for transfers between devices, on_device(): lax.all_gather(values, 'ctx', axis=0, tiled=True)  34.9 us
    dot_general x16, matrix products, work(): jnp.einsum('thd,nd->htn', queries, piece_k, preferred_element_type=jnp.fl...  26.9 us
    reduce_scatter x1, waiting for transfers between devices, on_device(): lax.psum_scatter(partial_value.astype(jnp.bfloat16), 'tp', scatter_dimens...  25.7 us
    dot_general x8, matrix products, work(): jnp.einsum('thd,nd->htn', grads3, piece_v, preferred_element_type=jnp.flo...  19.7 us
    dot_general x8, matrix products, work(): jnp.einsum('htn,nd->thd', ds_b, piece_k, preferred_element_type=jnp.float32)  13.9 us
  transfers between devices with their start and end apart: 5, of which 5 were waited for; matrix products, arithmetic and copies ran while one was open for 9% of the time, Pallas kernels for 0%

commit v1 on v0

--- a/solution.py
+++ b/solution.py
@@ -95,7 +95,9 @@
     zero_rows = jnp.zeros((seq, head_dim), jnp.float32)
     grad_init = (jnp.zeros((tokens, heads, head_dim), jnp.float32), zero_rows, zero_rows)
     all_keys, all_values = (
-        lax.all_gather(keys, "ctx", axis=0, tiled=True),
+        jnp.concatenate(
+            lax.all_to_all(jnp.stack([keys] * lax.axis_size("ctx")), "ctx", 0, 0), axis=0
+        ),
         lax.all_gather(values, "ctx", axis=0, tiled=True),
     )
     block = math.gcd(seq, 1024)

time: 590 us -> 534 us (0.905)
  waiting for transfers between devices: 410 us -> 342 us
  starting transfers between devices: 0.38 us -> 12.4 us
  matrix products: 108 us -> 100 us
  local copies, waits for them, and re-layouts: 6.58 us -> 12.8 us
    all_gather x1 -> x0, waiting for transfers between devices: 70.6 us -> none  [on_device(): lax.all_gather(keys, 'ctx', axis=0, tiled=True)]
    all_to_all x0 -> x1, waiting for transfers between devices: none -> 37 us  [on_device(): lax.all_to_all(jnp.stack([keys] * lax.axis_size('ctx')), 'ctx', 0, 0)]
    all_gather x1, waiting for transfers between devices: 34.9 us -> 0.02 us  [on_device(): lax.all_gather(values, 'ctx', axis=0, tiled=True)]
    all_to_all x0 -> x1, starting transfers between devices: none -> 12 us  [on_device(): lax.all_to_all(jnp.stack([keys] * lax.axis_size('ctx')), 'ctx', 0, 0)]
    dot_general x16, matrix products: 26.9 us -> 19.3 us  [work(): jnp.einsum('thd,nd->htn', queries, piece_k, preferred_element_type=jnp.fl...]
  transfers between devices with their start and end apart: 5 -> 5, of which waited for: 5 -> 4; matrix products, arithmetic and copies ran while one was open for 9% -> 9% of each run, Pallas kernels for 0% -> 0%
where the time goes in v1:
time: 534 us; the launch traced here: 532 us
  waiting for transfers between devices  342 us (64%)
  matrix products  100 us (19%)
  other arithmetic  30.7 us (6%)
  loops' own time  21.3 us (4%)
  between operations  13.3 us (2%)
  local copies, waits for them, and re-layouts  12.8 us (2%)
  starting transfers between devices  12.4 us (2%)
    reduce_scatter x1, waiting for transfers between devices, on_device(): lax.psum_scatter(dv_full, 'ctx', scatter_dimension=0, tiled=True)  145 us
    reduce_scatter x1, waiting for transfers between devices, on_device(): lax.psum_scatter(dk_full, 'ctx', scatter_dimension=0, tiled=True)  134 us
    all_to_all x1, waiting for transfers between devices, on_device(): lax.all_to_all(jnp.stack([keys] * lax.axis_size('ctx')), 'ctx', 0, 0)  37 us
    reduce_scatter x1, waiting for transfers between devices, on_device(): lax.psum_scatter(partial_value.astype(jnp.bfloat16), 'tp', scatter_dimens...  25.8 us
    dot_general x8, matrix products, work(): jnp.einsum('thd,nd->htn', grads3, piece_v, preferred_element_type=jnp.flo...  19.7 us
    dot_general x16, matrix products, work(): jnp.einsum('thd,nd->htn', queries, piece_k, preferred_element_type=jnp.fl...  19.3 us
    dot_general x8, matrix products, work(): jnp.einsum('htn,nd->thd', ds_b, piece_k, preferred_element_type=jnp.float32)  13.9 us
    dot_general x8, matrix products, work(): jnp.einsum('htn,thd->nd', p_b, grads3, preferred_element_type=jnp.float32)  13.3 us
  transfers between devices with their start and end apart: 5, of which 4 were waited for; matrix products, arithmetic and copies ran while one was open for 9% of the time, Pallas kernels for 0%

profile of v1, /device:TPU:2, one launch (start us, length us, event | category | flops | bytes accessed | tf_op | source)
XLA Modules:
  0.0 532.3 jit_solution(16171737559414458763)
XLA Ops:
  11.3 12.0 %all-to-all-start = ((bf16[64,128,128]{2,1,0:T(8,128)(2,1)}), bf16[64,128,128]{2,1,0:T(8,128)(2,1)S(1)}, u32[]{:S(2)}, u32[]{:S(2)}) async-start(bf16[64,128,128]{2,1,0:T(8,128)(2,1)} %stack.2), calls=%async_computation | async-start | bytes 4194304 | tf_op jit(solution)/shard_map/all_to_all | solution.py:99
  23.4 2.6 convolution_convert_fusion.1
  29.8 5.0 fusion.47
  36.8 37.0 %all-to-all-done = bf16[64,128,128]{2,1,0:T(8,128)(2,1)S(1)} async-done(((bf16[64,128,128]{2,1,0:T(8,128)(2,1)}), bf16[64,128,128]{2,1,0:T(8,128)(2,1)S(1)}, u32[]{:S(2)}, u32[]{:S(2)}) %all-to-all-start) | async-done | bytes 2097184 | tf_op jit(solution)/shard_map/all_to_all | solution.py:99
  73.8 35.5 %while.36 = (s32[]{:T(128)}, f32[8,128]{1,0:T(8,128)S(1)}, f32[8,128]{1,0:T(8,128)S(1)}, s32[128]{0:T(128)S(1)}, s32[]{:T(128)}, /*index=5*/s32[128]{0:T(128)S(1...) while((s32[]{:T(128)}, f32[8,128]{1,0:T(8,128)S(1)}, ...), condition=%wide.region_9.10_spmd, body=%wide.region_2.9_spmd.sunk | while | flops 277381120 | bytes 9385225 | solution.py:110
  85.1 2.0 conditional.4
  89.5 2.0 conditional.4
  110.7 2.2 broadcast_in_dim.148.clone
  113.0 2.2 broadcast_in_dim.148
  115.2 92.8 %while.37 = (s32[]{:T(128)}, f32[128,8,128]{2,0,1:T(8,128)S(1)}, f32[8192,128]{1,0:T(8,128)}, f32[8192,128]{1,0:T(8,128)}, s32[128]{0:T(128)S(1)}, /*index=5*/s3...) while((s32[]{:T(128)}, f32[128,8,128]{2,0,1:T(8,128)S(1)}, ...), condition=%wide.region_16.17_spmd, body=%wide.region_11.16_spmd.sunk | while | flops 1354397696 | bytes 23238016 | solution.py:121
  117.5 9.3 %conditional.5 = ((f32[128,8,128]{2,0,1:T(8,128)S(1)}, f32[8192,128]{1,0:T(8,128)}, f32[8192,128]{1,0:T(8,128)})) conditional(s32[]{:T(128)} %convert_element_type.94, (s32[1024]{0:T(1024)S(1)}, s32[128]{0:T(128)S(1)}, s32[]{:T(128)}, bf16[8192,128]{1,0:T(8,128)(2,1)}, bf16[128,8,128]{2,0,1:T(8,128)(2,1)S(1)}, /*index=5*/f32[8,128]{1,0:T(8,128)S(1)}, ...), branch_computations={%region_14.14_spmd, %region_15.15_spmd} | conditional | flops 1353973760 | bytes 23216726 | solution.py:50
  119.4 2.5 fusion.13
  129.1 9.3 %conditional.5 = ((f32[128,8,128]{2,0,1:T(8,128)S(1)}, f32[8192,128]{1,0:T(8,128)}, f32[8192,128]{1,0:T(8,128)})) conditional(s32[]{:T(128)} %convert_element_type.94, (s32[1024]{0:T(1024)S(1)}, s32[128]{0:T(128)S(1)}, s32[]{:T(128)}, bf16[8192,128]{1,0:T(8,128)(2,1)}, bf16[128,8,128]{2,0,1:T(8,128)(2,1)S(1)}, /*index=5*/f32[8,128]{1,0:T(8,128)S(1)}, ...), branch_computations={%region_14.14_spmd, %region_15.15_spmd} | conditional | flops 1353973760 | bytes 23216726 | solution.py:50
  131.0 2.5 fusion.13
  140.7 9.3 %conditional.5 = ((f32[128,8,128]{2,0,1:T(8,128)S(1)}, f32[8192,128]{1,0:T(8,128)}, f32[8192,128]{1,0:T(8,128)})) conditional(s32[]{:T(128)} %convert_element_type.94, (s32[1024]{0:T(1024)S(1)}, s32[128]{0:T(128)S(1)}, s32[]{:T(128)}, bf16[8192,128]{1,0:T(8,128)(2,1)}, bf16[128,8,128]{2,0,1:T(8,128)(2,1)S(1)}, /*index=5*/f32[8,128]{1,0:T(8,128)S(1)}, ...), branch_computations={%region_14.14_spmd, %region_15.15_spmd} | conditional | flops 1353973760 | bytes 23216726 | solution.py:50
  142.6 2.5 fusion.13
  152.3 9.3 %conditional.5 = ((f32[128,8,128]{2,0,1:T(8,128)S(1)}, f32[8192,128]{1,0:T(8,128)}, f32[8192,128]{1,0:T(8,128)})) conditional(s32[]{:T(128)} %convert_element_type.94, (s32[1024]{0:T(1024)S(1)}, s32[128]{0:T(128)S(1)}, s32[]{:T(128)}, bf16[8192,128]{1,0:T(8,128)(2,1)}, bf16[128,8,128]{2,0,1:T(8,128)(2,1)S(1)}, /*index=5*/f32[8,128]{1,0:T(8,128)S(1)}, ...), branch_computations={%region_14.14_spmd, %region_15.15_spmd} | conditional | flops 1353973760 | bytes 23216726 | solution.py:50
  154.2 2.5 fusion.13
  163.9 9.3 %conditional.5 = ((f32[128,8,128]{2,0,1:T(8,128)S(1)}, f32[8192,128]{1,0:T(8,128)}, f32[8192,128]{1,0:T(8,128)})) conditional(s32[]{:T(128)} %convert_element_type.94, (s32[1024]{0:T(1024)S(1)}, s32[128]{0:T(128)S(1)}, s32[]{:T(128)}, bf16[8192,128]{1,0:T(8,128)(2,1)}, bf16[128,8,128]{2,0,1:T(8,128)(2,1)S(1)}, /*index=5*/f32[8,128]{1,0:T(8,128)S(1)}, ...), branch_computations={%region_14.14_spmd, %region_15.15_spmd} | conditional | flops 1353973760 | bytes 23216726 | solution.py:50
  165.8 2.5 fusion.13
  175.5 9.3 %conditional.5 = ((f32[128,8,128]{2,0,1:T(8,128)S(1)}, f32[8192,128]{1,0:T(8,128)}, f32[8192,128]{1,0:T(8,128)})) conditional(s32[]{:T(128)} %convert_element_type.94, (s32[1024]{0:T(1024)S(1)}, s32[128]{0:T(128)S(1)}, s32[]{:T(128)}, bf16[8192,128]{1,0:T(8,128)(2,1)}, bf16[128,8,128]{2,0,1:T(8,128)(2,1)S(1)}, /*index=5*/f32[8,128]{1,0:T(8,128)S(1)}, ...), branch_computations={%region_14.14_spmd, %region_15.15_spmd} | conditional | flops 1353973760 | bytes 23216726 | solution.py:50
  177.4 2.5 fusion.13
  187.1 9.2 %conditional.5 = ((f32[128,8,128]{2,0,1:T(8,128)S(1)}, f32[8192,128]{1,0:T(8,128)}, f32[8192,128]{1,0:T(8,128)})) conditional(s32[]{:T(128)} %convert_element_type.94, (s32[1024]{0:T(1024)S(1)}, s32[128]{0:T(128)S(1)}, s32[]{:T(128)}, bf16[8192,128]{1,0:T(8,128)(2,1)}, bf16[128,8,128]{2,0,1:T(8,128)(2,1)S(1)}, /*index=5*/f32[8,128]{1,0:T(8,128)S(1)}, ...), branch_computations={%region_14.14_spmd, %region_15.15_spmd} | conditional | flops 1353973760 | bytes 23216726 | solution.py:50
  189.0 2.5 fusion.13
  198.7 9.3 %conditional.5 = ((f32[128,8,128]{2,0,1:T(8,128)S(1)}, f32[8192,128]{1,0:T(8,128)}, f32[8192,128]{1,0:T(8,128)})) conditional(s32[]{:T(128)} %convert_element_type.94, (s32[1024]{0:T(1024)S(1)}, s32[128]{0:T(128)S(1)}, s32[]{:T(128)}, bf16[8192,128]{1,0:T(8,128)(2,1)}, bf16[128,8,128]{2,0,1:T(8,128)(2,1)S(1)}, /*index=5*/f32[8,128]{1,0:T(8,128)S(1)}, ...), branch_computations={%region_14.14_spmd, %region_15.15_spmd} | conditional | flops 1353973760 | bytes 23216726 | solution.py:50
  200.6 2.5 fusion.13
  209.0 7.7 %fusion.58 = f32[128,4096]{1,0:T(8,128)} fusion(bf16[128,1024]{0,1:T(8,128)(2,1)S(1)} %bitcast.87, bf16[4096,1024]{1,0:T(8,128)(2,1)} %param.16), kind=kOutput, calls=%fused_computation.93 | convolution fusion | flops 1073741824 | bytes 10747904 | tf_op jit(solution)/shard_map/dot_general | solution.py:21
  216.7 133.7 %reduce-scatter.4.cloned.1.call-done = f32[128,128]{1,0:T(8,128)} async-done(((f32[8192,128]{1,0:T(8,128)}), f32[128,128]{1,0:T(8,128)}) %reduce-scatter.4.cloned.1.call-update) | async-done | bytes 65552 | tf_op jit(solution)/shard_map/reduce_scatter | solution.py:123
  350.4 2.1 convolution_add_fusion.1
  352.4 144.8 %reduce-scatter.6.cloned.1.call-done = f32[128,128]{1,0:T(8,128)} async-done(((f32[8192,128]{1,0:T(8,128)}), f32[128,128]{1,0:T(8,128)}) %reduce-scatter.6.cloned.1.call-update) | async-done | bytes 65552 | tf_op jit(solution)/shard_map/reduce_scatter | solution.py:124
  497.3 2.7 fusion.46
  500.0 25.8 %reduce-scatter.8.cloned.1.call-done = bf16[128,1024]{1,0:T(8,128)(2,1)} async-done(((bf16[128,4096]{1,0:T(8,128)(2,1)}), bf16[128,1024]{1,0:T(8,128)(2,1)}) %reduce-scatter.8.cloned.1.call-update) | async-done | bytes 262160 | tf_op jit(solution)/shard_map/reduce_scatter | solution.py:130
  (176 shorter events, 112.5 us)
Async XLA Ops:
  6.5 1.2 copy-start
  11.3 62.6 %all-to-all-start = ((bf16[64,128,128]{2,1,0:T(8,128)(2,1)}), bf16[64,128,128]{2,1,0:T(8,128)(2,1)S(1)}, u32[]{:S(2)}, u32[]{:S(2)}) async-start(bf16[64,128,128]{2,1,0:T(8,128)(2,1)} %stack.2), calls=%async_computation | async-start | bytes 4194304 | tf_op jit(solution)/shard_map/all_to_all | solution.py:99
  23.3 86.1 %all-gather.2.cloned.1.call-start = ((), (), s32[]{:S(2)}) async-start(), calls=%async_computation.4 | async-start | bytes 2129920 | tf_op jit(solution)/shard_map/all_gather | solution.py:101
  25.9 324.4 %reduce-scatter.4.cloned.1.call-start = ((), (), s32[]{:S(2)}) async-start(), calls=%async_computation.5 | async-start | bytes 4259840 | tf_op jit(solution)/shard_map/reduce_scatter | solution.py:123
  27.1 2.7 copy-start.2
  29.8 5.1 copy-start.4
  109.4 1.3 copy-start.1
  110.7 4.5 copy-start.3
  208.0 289.2 %reduce-scatter.6.cloned.1.call-start = ((), (), s32[]{:S(2)}) async-start(), calls=%async_computation.6 | async-start | bytes 4259840 | tf_op jit(solution)/shard_map/reduce_scatter | solution.py:124
  208.8 317.0 %reduce-scatter.8.cloned.1.call-start = ((), (), s32[]{:S(2)}) async-start(), calls=%async_computation.7 | async-start | bytes 1310720 | tf_op jit(solution)/shard_map/reduce_scatter | solution.py:130
Sparse Core Ops, SparseCore 0:
  26.9 79.6 all-gather.1
  208.1 142.1 reduce-scatter.3
  354.5 142.7 reduce-scatter.5
  500.1 25.5 reduce-scatter.7
